TPU v7x, 512 devices: a whole 4x8x8 slice. The times are simulated.
512 devices in a mesh: expert: 64 (over x, z, core), group: 8 (over y).
Axes of the slice: x: 4, y: 8, z: 8, core: 2. Of those that a mesh axis runs over, the one named last changes fastest.
Arguments:
- tokens: bfloat16 [4096, 4096], P('expert', 'group'), may hold values from -6 to 6
- gate_weight: bfloat16 [64, 1536, 4096], P('expert', 'group'), may hold values from -0.09375 to 0.09375
- up_weight: bfloat16 [64, 1536, 4096], P('expert', 'group'), may hold values from -0.09375 to 0.09375
- down_weight: bfloat16 [64, 1536, 4096], P('expert', 'group'), may hold values from -0.15625 to 0.15625
- expert_ids: int32 [4096, 8], P('expert'), may hold values from 0 to 63, all different within a row; in each aligned block of 64 rows (0 to 63, 64 to 127, ...) at most 12 rows name the same one
- gate_scores: bfloat16 [4096, 8], P('expert'), may hold values from 0.19921875 to 1
Outputs:
- mixed: bfloat16 [4096, 4096], P('expert', 'group')
Inputs may be any that keep to these rules, and one draw needn't show every extreme that they name: `expert_ids`: the 8 experts of a token are distinct; within the 64 rows of one device no expert is named by more than 12 rows, a bound that some block reaches.
All inputs are finite; a program needn't handle non-finite values.
Results may differ from a plain program's by a relative error of at most 0.019.
Values may be sent and summed in bfloat16 or wider, within the bound.
No kernel may reach another device: no remote copies, remote signals or barrier semaphores. Data moves between devices by JAX's collectives and lax.ppermute only.
A program may use at most 128 MiB of HBM per device.

v0:
```python
import jax
import jax.numpy as jnp
from jax import lax
from jax.sharding import PartitionSpec as P


def per_device(tokens, gate_weight, up_weight, down_weight, expert_ids, gate_scores):
    experts = lax.axis_size("expert")
    tok_rows = tokens.shape[0]
    top_count = expert_ids.shape[1]
    capacity = tok_rows * top_count * 3 // (2 * experts)
    flat_ids = expert_ids.reshape(-1)
    onehot = (flat_ids[:, None] == jnp.arange(experts, dtype=jnp.int32)[None, :]).astype(jnp.int32)
    before = jnp.cumsum(onehot, axis=0) - onehot
    slot_index = jnp.sum(before * onehot, axis=1).reshape(tok_rows, top_count)
    slot_keys = expert_ids * capacity + slot_index
    columns = jnp.arange(experts * capacity, dtype=jnp.int32)
    matches = slot_keys[:, :, None] == columns[None, None, :]
    selector = jnp.any(matches, axis=1).astype(jnp.bfloat16)
    weights = jnp.sum(
        jnp.where(matches, gate_scores[:, :, None].astype(jnp.float32), 0.0), axis=1
    ).astype(jnp.bfloat16)
    whole_rows = lax.all_gather(tokens, "group", axis=1, tiled=True)
    placed = lax.dot_general(
        selector, whole_rows, (((0,), (0,)), ((), ())), preferred_element_type=jnp.float32
    )
    arrived = lax.all_to_all(
        placed.astype(jnp.bfloat16).reshape(experts, capacity, whole_rows.shape[1]),
        "expert",
        split_axis=0,
        concat_axis=0,
        tiled=True,
    )
    row_block = arrived.reshape(-1, arrived.shape[2])
    gate_value = lax.dot_general(
        row_block, gate_weight[0], (((1,), (1,)), ((), ())), preferred_element_type=jnp.float32
    )
    up_value = lax.dot_general(
        row_block, up_weight[0], (((1,), (1,)), ((), ())), preferred_element_type=jnp.float32
    )
    hidden = (jax.nn.silu(gate_value) * up_value).astype(jnp.bfloat16)
    partial_value = jnp.dot(hidden, down_weight[0], preferred_element_type=jnp.float32)
    returned = lax.all_to_all(
        partial_value.astype(jnp.bfloat16).reshape(arrived.shape),
        "expert",
        split_axis=0,
        concat_axis=0,
        tiled=True,
    )
    combined = jnp.dot(
        weights, returned.reshape(experts * capacity, -1), preferred_element_type=jnp.float32
    )
    return lax.psum_scatter(combined.astype(jnp.bfloat16), "group", scatter_dimension=1, tiled=True)


def solution(mesh):
    placed = (
        P("expert", "group"),
        P("expert", "group", None),
        P("expert", "group", None),
        P("expert", "group", None),
        P("expert", None),
        P("expert", None),
    )
    return jax.shard_map(
        per_device, mesh=mesh, in_specs=placed, out_specs=P("expert", "group"), check_vma=False
    )
```

profile of v0, /device:TPU:2, one launch (start us, length us, event | category | flops | bytes accessed | tf_op | source)
XLA Modules:
  0.0 540.2 jit_solution(18164312794375199998)
XLA Ops:
  6.5 0.0 copy-start
  6.5 0.9 copy.21
  7.4 0.1 eq.42
  7.5 0.1 eq.38
  7.6 1.2 reduce-window.6
  8.8 0.2 slice_reduce_fusion
  9.1 0.1 fusion.22
  9.2 0.1 reshape.36
  9.3 0.1 copy.24
  9.4 0.7 multiply_add_fusion
  10.1 0.1 copy.25
  10.2 0.5 fusion.5
  10.7 27.1 %all_gather.3 = bf16[64,4096]{1,0:T(8,128)(2,1)S(1)} all-gather(bf16[64,512]{1,0:T(8,128)(2,1)} %param.6), channel_id=1, replica_groups=mesh['expert'=64,'group'=8] {'group'}, dimensions={1}, use_global_device_ids=true | all-gather | bytes 589824 | tf_op jit(solution)/shard_map/all_gather | solution.py:23
  37.9 4.6 convolution_convert_fusion
  42.4 9.8 %reshape.37 = bf16[64,12,4096]{2,1,0:T(8,128)(2,1)} reshape(bf16[768,4096]{1,0:T(8,128)(2,1)} %convolution_convert_fusion) | data formatting | bytes 12582912 | tf_op jit(solution)/shard_map/reshape | solution.py:28
  52.2 198.1 %all_to_all.10 = bf16[64,12,4096]{2,1,0:T(8,128)(2,1)} all-to-all(bf16[64,12,4096]{2,1,0:T(8,128)(2,1)} %reshape.37), channel_id=1, replica_groups=mesh['expert'=64,'group'=8] {'expert'}, dimensions={0} | all-to-all | bytes 12582912 | tf_op jit(solution)/shard_map/all_to_all | solution.py:27
  250.3 0.0 copy-start.2
  250.3 10.1 %reshape.38 = bf16[768,4096]{1,0:T(8,128)(2,1)} reshape(bf16[64,12,4096]{2,1,0:T(8,128)(2,1)} %all_to_all.10) | data formatting | bytes 12582912 | tf_op jit(solution)/shard_map/reshape | solution.py:34
  260.4 0.0 copy-done.2
  260.4 5.8 %fusion.3 = f32[768,192]{0,1:T(8,128)} fusion(bf16[768,4096]{1,0:T(8,128)(2,1)} %reshape.38, bf16[1,192,4096]{2,1,0:T(8,128)(2,1)S(1)} %copy-done.2), kind=kOutput, calls=%fused_computation.6 | convolution fusion | flops 1207959552 | bytes 8454144 | tf_op jit(solution)/shard_map/dot_general | solution.py:35
  266.3 0.0 copy-done
  266.3 13.5 %convolution_convert_fusion.1 = bf16[768,4096]{1,0:T(8,128)(2,1)} fusion(bf16[1,192,4096]{2,1,0:T(8,128)(2,1)S(1)} %copy-done, bf16[768,4096]{1,0:T(8,128)(2,1)} %reshape.38, bf16[1,192,4096]{2,1,0:T(8,128)(2,1)} %param.8, f32[768,192]{0,1:T(8,128)} %fusion.3), kind=kOutput, calls=%fused_computation.1 | convolution fusion | flops 2419949568 | bytes 16318464 | tf_op jit(solution)/shard_map/dot_general | solution.py:42
  279.7 9.8 %reshape.39 = bf16[64,12,4096]{2,1,0:T(8,128)(2,1)} reshape(bf16[768,4096]{1,0:T(8,128)(2,1)} %convolution_convert_fusion.1) | data formatting | bytes 12582912 | tf_op jit(solution)/shard_map/reshape | solution.py:44
  289.5 0.0 copy-start.1
  289.5 8.0 %all-to-all-start.1 = ((bf16[64,12,4096]{2,1,0:T(8,128)(2,1)}), bf16[64,12,4096]{2,1,0:T(8,128)(2,1)}, u32[]{:S(2)}, u32[]{:S(2)}) async-start(bf16[64,12,4096]{2,1,0:T(8,128)(2,1)} %reshape.39), calls=%async_computation.1 | async-start | bytes 16777216 | tf_op jit(solution)/shard_map/all_to_all | solution.py:43
  297.6 0.0 reduce-scatter.2.cloned.1.call-start
  297.6 0.0 copy-done.1
  297.6 0.1 copy.26
  297.7 0.6 select_reduce_fusion
  298.3 183.5 %all-to-all-done.1 = bf16[64,12,4096]{2,1,0:T(8,128)(2,1)} async-done(((bf16[64,12,4096]{2,1,0:T(8,128)(2,1)}), bf16[64,12,4096]{2,1,0:T(8,128)(2,1)}, u32[]{:S(2)}, u32[]{:S(2)}) %all-to-all-start.1) | async-done | bytes 6291488 | tf_op jit(solution)/shard_map/all_to_all | solution.py:43
  481.8 9.9 %reshape.40 = bf16[768,4096]{1,0:T(8,128)(2,1)} reshape(bf16[64,12,4096]{2,1,0:T(8,128)(2,1)} %all-to-all-done.1) | data formatting | bytes 12582912 | tf_op jit(solution)/shard_map/reshape | solution.py:51
  491.6 4.8 convolution_convert_fusion.2
  496.4 0.0 reduce-scatter.2.cloned.1.call-update
  496.5 36.9 %reduce-scatter.2.cloned.1.call-done = bf16[64,512]{1,0:T(8,128)(2,1)} async-done(((bf16[64,4096]{1,0:T(8,128)(2,1)}), bf16[64,512]{1,0:T(8,128)(2,1)}) %reduce-scatter.2.cloned.1.call-update) | async-done | bytes 65552 | tf_op jit(solution)/shard_map/reduce_scatter | solution.py:53
  (3 shorter events, 0.1 us)
Async XLA Ops:
  6.5 259.7 %copy-start = (bf16[1,192,4096]{2,1,0:T(8,128)(2,1)S(1)}, bf16[1,192,4096]{2,1,0:T(8,128)(2,1)}, u32[]{:S(2)}) copy-start(bf16[1,192,4096]{2,1,0:T(8,128)(2,1)} %param.9) | copy-start | bytes 4718596
  250.3 10.1 %copy-start.2 = (bf16[1,192,4096]{2,1,0:T(8,128)(2,1)S(1)}, bf16[1,192,4096]{2,1,0:T(8,128)(2,1)}, u32[]{:S(2)}) copy-start(bf16[1,192,4096]{2,1,0:T(8,128)(2,1)} %param.7) | copy-start | bytes 4718596
  289.5 8.1 %copy-start.1 = (bf16[64,8]{0,1:T(8,128)(2,1)S(1)}, bf16[64,8]{0,1:T(8,128)(2,1)}, u32[]{:S(2)}) copy-start(bf16[64,8]{0,1:T(8,128)(2,1)} %param.11) | copy-start | bytes 3076
  289.5 192.3 %all-to-all-start.1 = ((bf16[64,12,4096]{2,1,0:T(8,128)(2,1)}), bf16[64,12,4096]{2,1,0:T(8,128)(2,1)}, u32[]{:S(2)}, u32[]{:S(2)}) async-start(bf16[64,12,4096]{2,1,0:T(8,128)(2,1)} %reshape.39), calls=%async_computation.1 | async-start | bytes 16777216 | tf_op jit(solution)/shard_map/all_to_all | solution.py:43
  297.6 235.8 %reduce-scatter.2.cloned.1.call-start = ((), (), s32[]{:S(2)}) async-start(), calls=%async_computation.3 | async-start | bytes 589824 | tf_op jit(solution)/shard_map/reduce_scatter | solution.py:53
Sparse Core Ops, SparseCore 0:
  496.6 36.7 reduce-scatter.1
where the time goes:
time: 541 us; the launch traced here: 540 us
  blocking collectives  225 us (42%)
  waiting for transfers between devices  220 us (41%)
  local copies, waits for them, and re-layouts  41.1 us (8%)
  matrix products  28.6 us (5%)
  between operations  13.5 us (2%)
  starting transfers between devices  8.08 us (1%)
    all_to_all x1, blocking collectives, per_device(): lax.all_to_all(placed.astype(jnp.bfloat16).reshape(experts, capacity, who...  198 us
    all_to_all x1, waiting for transfers between devices, per_device(): lax.all_to_all(partial_value.astype(jnp.bfloat16).reshape(arrived.shape),...  184 us
    reduce_scatter x1, waiting for transfers between devices, per_device(): lax.psum_scatter(combined.astype(jnp.bfloat16), 'group', scatter_dimensio...  36.9 us
    all_gather x1, blocking collectives, per_device(): whole_rows = lax.all_gather(tokens, 'group', axis=1, tiled=True)  27.1 us
    dot_general x1, matrix products, per_device(): jnp.dot(hidden, down_weight[0], preferred_element_type=jnp.float32)  13.5 us
  transfers between devices with their start and end apart: 2, of which 2 were waited for; matrix products, arithmetic and copies ran while one was open for 0% of the time, Pallas kernels for 0%

commit v1 on v0

--- a/solution.py
+++ b/solution.py
@@ -2,6 +2,12 @@
 import jax.numpy as jnp
 from jax import lax
 from jax.sharding import PartitionSpec as P
+
+
+def gather_from_all(x, axis, dim):
+    count = lax.axis_size(axis)
+    repeats = [count if d == dim else 1 for d in range(x.ndim)]
+    return lax.all_to_all(jnp.tile(x, repeats), axis, split_axis=dim, concat_axis=dim, tiled=True)
 
 
 def per_device(tokens, gate_weight, up_weight, down_weight, expert_ids, gate_scores):
@@ -20,7 +26,7 @@
     weights = jnp.sum(
         jnp.where(matches, gate_scores[:, :, None].astype(jnp.float32), 0.0), axis=1
     ).astype(jnp.bfloat16)
-    whole_rows = lax.all_gather(tokens, "group", axis=1, tiled=True)
+    whole_rows = gather_from_all(tokens, "group", 1)
     placed = lax.dot_general(
         selector, whole_rows, (((0,), (0,)), ((), ())), preferred_element_type=jnp.float32
     )

time: 541 us -> 532 us (0.983)
  blocking collectives: 225 us -> 198 us
  waiting for transfers between devices: 220 us -> 230 us
  starting transfers between devices: 8.08 us -> 15.2 us
    all_gather x1 -> x0, blocking collectives: 27.1 us -> none  [per_device(): whole_rows = lax.all_gather(tokens, 'group', axis=1, tiled=True)]
    all_to_all x0 -> x1, waiting for transfers between devices: none -> 13.4 us  [gather_from_all(): lax.all_to_all(jnp.tile(x, repeats), axis, split_axis=dim, concat_axis=di...]
    all_to_all x0 -> x1, starting transfers between devices: none -> 7.1 us  [gather_from_all(): lax.all_to_all(jnp.tile(x, repeats), axis, split_axis=dim, concat_axis=di...]
  transfers between devices with their start and end apart: 2 -> 3, of which waited for: 2 -> 3; matrix products, arithmetic and copies ran while one was open for 0% -> 1% of each run, Pallas kernels for 0% -> 0%
where the time goes in v1:
time: 532 us; the launch traced here: 531 us
  waiting for transfers between devices  230 us (43%)
  blocking collectives  198 us (37%)
  local copies, waits for them, and re-layouts  42.7 us (8%)
  matrix products  28 us (5%)
  starting transfers between devices  15.2 us (3%)
  between operations  13.5 us (3%)
    all_to_all x1, blocking collectives, per_device(): lax.all_to_all(placed.astype(jnp.bfloat16).reshape(experts, capacity, who...  198 us
    all_to_all x1, waiting for transfers between devices, per_device(): lax.all_to_all(partial_value.astype(jnp.bfloat16).reshape(arrived.shape),...  184 us
    reduce_scatter x1, waiting for transfers between devices, per_device(): lax.psum_scatter(combined.astype(jnp.bfloat16), 'group', scatter_dimensio...  33 us
    all_to_all x1, waiting for transfers between devices, gather_from_all(): lax.all_to_all(jnp.tile(x, repeats), axis, split_axis=dim, concat_axis=di...  13.4 us
    dot_general x1, matrix products, per_device(): jnp.dot(hidden, down_weight[0], preferred_element_type=jnp.float32)  13.3 us
  transfers between devices with their start and end apart: 3, of which 3 were waited for; matrix products, arithmetic and copies ran while one was open for 1% of the time, Pallas kernels for 0%

profile of v1, /device:TPU:2, one launch (start us, length us, event | category | flops | bytes accessed | tf_op | source)
XLA Modules:
  0.0 530.7 jit_solution(7177577532529289477)
XLA Ops:
  6.5 0.0 copy-start
  6.5 1.8 tile.2
  8.3 7.1 %all-to-all-start = ((bf16[64,8,512]{2,0,1:T(8,128)(2,1)}), bf16[64,8,512]{2,0,1:T(8,128)(2,1)S(1)}, u32[]{:S(2)}, u32[]{:S(2)}) async-start(bf16[64,8,512]{2,0,1:T(8,128)(2,1)} %tile.2), calls=%async_computation | async-start | bytes 1048576 | tf_op jit(solution)/shard_map/all_to_all | solution.py:10
  15.4 0.8 copy.35
  16.2 0.1 eq.42
  16.3 0.1 eq.38
  16.4 1.2 reduce-window.6
  17.6 0.2 slice_reduce_fusion
  17.9 0.1 fusion.22
  18.0 0.1 reshape.43
  18.1 0.1 copy.38
  18.2 0.7 multiply_add_fusion
  18.9 0.1 copy.39
  19.0 0.5 fusion.5
  19.5 13.4 %all-to-all-done = bf16[64,8,512]{2,0,1:T(8,128)(2,1)S(1)} async-done(((bf16[64,8,512]{2,0,1:T(8,128)(2,1)}), bf16[64,8,512]{2,0,1:T(8,128)(2,1)S(1)}, u32[]{:S(2)}, u32[]{:S(2)}) %all-to-all-start) | async-done | bytes 524320 | tf_op jit(solution)/shard_map/all_to_all | solution.py:10
  33.0 4.6 convolution_convert_fusion
  37.5 9.8 %reshape.44 = bf16[64,12,4096]{2,1,0:T(8,128)(2,1)} reshape(bf16[768,4096]{1,0:T(8,128)(2,1)} %convolution_convert_fusion) | data formatting | bytes 12582912 | tf_op jit(solution)/shard_map/reshape | solution.py:34
  47.3 198.1 %all_to_all.19 = bf16[64,12,4096]{2,1,0:T(8,128)(2,1)} all-to-all(bf16[64,12,4096]{2,1,0:T(8,128)(2,1)} %reshape.44), channel_id=1, replica_groups=mesh['expert'=64,'group'=8] {'expert'}, dimensions={0} | all-to-all | bytes 12582912 | tf_op jit(solution)/shard_map/all_to_all | solution.py:33
  245.4 10.0 %reshape.45 = bf16[768,4096]{1,0:T(8,128)(2,1)} reshape(bf16[64,12,4096]{2,1,0:T(8,128)(2,1)} %all_to_all.19) | data formatting | bytes 12582912 | tf_op jit(solution)/shard_map/reshape | solution.py:40
  255.4 5.4 %fusion.3 = f32[768,192]{0,1:T(8,128)S(1)} fusion(bf16[768,4096]{1,0:T(8,128)(2,1)} %reshape.45, bf16[1,192,4096]{2,1,0:T(8,128)(2,1)} %param.7), kind=kOutput, calls=%fused_computation.6 | convolution fusion | flops 1207959552 | bytes 8454144 | tf_op jit(solution)/shard_map/dot_general | solution.py:41
  260.8 0.0 copy-done
  260.8 13.3 %convolution_convert_fusion.1 = bf16[768,4096]{1,0:T(8,128)(2,1)} fusion(bf16[1,192,4096]{2,1,0:T(8,128)(2,1)S(1)} %copy-done, bf16[768,4096]{1,0:T(8,128)(2,1)} %reshape.45, bf16[1,192,4096]{2,1,0:T(8,128)(2,1)} %param.8, f32[768,192]{0,1:T(8,128)S(1)} %fusion.3), kind=kOutput, calls=%fused_computation.1 | convolution fusion | flops 2419949568 | bytes 16318464 | tf_op jit(solution)/shard_map/dot_general | solution.py:48
  274.1 9.7 %reshape.46 = bf16[64,12,4096]{2,1,0:T(8,128)(2,1)} reshape(bf16[768,4096]{1,0:T(8,128)(2,1)} %convolution_convert_fusion.1) | data formatting | bytes 12582912 | tf_op jit(solution)/shard_map/reshape | solution.py:50
  283.8 0.0 copy-start.1
  283.9 8.1 %all-to-all-start.2 = ((bf16[64,12,4096]{2,1,0:T(8,128)(2,1)}), bf16[64,12,4096]{2,1,0:T(8,128)(2,1)}, u32[]{:S(2)}, u32[]{:S(2)}) async-start(bf16[64,12,4096]{2,1,0:T(8,128)(2,1)} %reshape.46), calls=%async_computation.2 | async-start | bytes 16777216 | tf_op jit(solution)/shard_map/all_to_all | solution.py:49
  291.9 0.0 reduce-scatter.2.cloned.1.call-start
  292.0 0.0 copy-done.1
  292.0 0.1 copy.40
  292.1 0.6 select_reduce_fusion
  292.6 183.5 %all-to-all-done.2 = bf16[64,12,4096]{2,1,0:T(8,128)(2,1)} async-done(((bf16[64,12,4096]{2,1,0:T(8,128)(2,1)}), bf16[64,12,4096]{2,1,0:T(8,128)(2,1)}, u32[]{:S(2)}, u32[]{:S(2)}) %all-to-all-start.2) | async-done | bytes 6291488 | tf_op jit(solution)/shard_map/all_to_all | solution.py:49
  476.2 9.9 %reshape.47 = bf16[768,4096]{1,0:T(8,128)(2,1)} reshape(bf16[64,12,4096]{2,1,0:T(8,128)(2,1)} %all-to-all-done.2) | data formatting | bytes 12582912 | tf_op jit(solution)/shard_map/reshape | solution.py:57
  486.0 4.8 convolution_convert_fusion.2
  490.8 0.0 reduce-scatter.2.cloned.1.call-update
  490.8 33.0 %reduce-scatter.2.cloned.1.call-done = bf16[64,512]{1,0:T(8,128)(2,1)} async-done(((bf16[64,4096]{1,0:T(8,128)(2,1)}), bf16[64,512]{1,0:T(8,128)(2,1)}) %reduce-scatter.2.cloned.1.call-update) | async-done | bytes 65552 | tf_op jit(solution)/shard_map/reduce_scatter | solution.py:59
  (4 shorter events, 0.1 us)
Async XLA Ops:
  6.5 254.3 %copy-start = (bf16[1,192,4096]{2,1,0:T(8,128)(2,1)S(1)}, bf16[1,192,4096]{2,1,0:T(8,128)(2,1)}, u32[]{:S(2)}) copy-start(bf16[1,192,4096]{2,1,0:T(8,128)(2,1)} %param.9) | copy-start | bytes 4718596
  8.3 24.6 %all-to-all-start = ((bf16[64,8,512]{2,0,1:T(8,128)(2,1)}), bf16[64,8,512]{2,0,1:T(8,128)(2,1)S(1)}, u32[]{:S(2)}, u32[]{:S(2)}) async-start(bf16[64,8,512]{2,0,1:T(8,128)(2,1)} %tile.2), calls=%async_computation | async-start | bytes 1048576 | tf_op jit(solution)/shard_map/all_to_all | solution.py:10
  283.8 8.1 %copy-start.1 = (bf16[64,8]{0,1:T(8,128)(2,1)S(1)}, bf16[64,8]{0,1:T(8,128)(2,1)}, u32[]{:S(2)}) copy-start(bf16[64,8]{0,1:T(8,128)(2,1)} %param.11) | copy-start | bytes 3076
  283.9 192.3 %all-to-all-start.2 = ((bf16[64,12,4096]{2,1,0:T(8,128)(2,1)}), bf16[64,12,4096]{2,1,0:T(8,128)(2,1)}, u32[]{:S(2)}, u32[]{:S(2)}) async-start(bf16[64,12,4096]{2,1,0:T(8,128)(2,1)} %reshape.46), calls=%async_computation.2 | async-start | bytes 16777216 | tf_op jit(solution)/shard_map/all_to_all | solution.py:49
  291.9 231.9 %reduce-scatter.2.cloned.1.call-start = ((), (), s32[]{:S(2)}) async-start(), calls=%async_computation.4 | async-start | bytes 589824 | tf_op jit(solution)/shard_map/reduce_scatter | solution.py:59
Sparse Core Ops, SparseCore 0:
  490.9 32.8 reduce-scatter.1
